TPU v7x, 32 devices: a whole 2x2x4 slice. The times are simulated.
32 devices in a mesh: grp: 4 (over y, core), shard: 8 (over z, x).
Axes of the slice: x: 2, y: 2, z: 4, core: 2. Of those that a mesh axis runs over, the one named last changes fastest.
Arguments:
- query_rows: bfloat16 [16, 6144], P('grp'), may hold values from -10 to 10
- key_cache: bfloat16 [16, 2048, 1024], P('grp', 'shard'), may hold values from -10 to 10
- value_cache: bfloat16 [16, 2048, 1024], P('grp', 'shard'), may hold values from -6 to 6
- lengths: int32 [16], P('grp'), may hold values from 2 to 2048
- attn_gain: float32 [6144], replicated, may hold values from 0.5 to 1.5
- router: bfloat16 [6144, 4], replicated, may hold values from -0.078125 to 0.078125
- expert_ids: int32 [16, 2], replicated, may hold values from 0 to 3, all different within a row; in each aligned block of 4 rows (0 to 3, 4 to 7, ...) at most 2 rows name the same one
- w_gate: bfloat16 [4, 6144, 8192], P('grp', None, 'shard'), may hold values from -0.078125 to 0.078125
- w_up: bfloat16 [4, 6144, 8192], P('grp', None, 'shard'), may hold values from -0.078125 to 0.078125
- w_down: bfloat16 [4, 8192, 6144], P('grp', 'shard'), may hold values from -0.0625 to 0.0625
Outputs:
- normed: bfloat16 [16, 6144], P('grp')
- expert_out: bfloat16 [16, 6144], P('grp', 'shard')
Inputs may be any that keep to these rules, and one draw needn't show every extreme that they name: `expert_ids`: the two ids of a row differ. Among the 4 rows of one index of grp (aligned blocks), no expert is named by more than 2 rows, a bound that some block reaches.
All inputs are finite; a program needn't handle non-finite values.
Results may differ from a plain program's by a relative error of at most 0.0095.
Values may be sent and summed in bfloat16 or wider, within the bound.
No kernel may reach another device: no remote copies, remote signals or barrier semaphores. Data moves between devices by JAX's collectives and lax.ppermute only.
A program may use at most 128 MiB of HBM per device.

v0:
```python
import math
import jax
import jax.numpy as jnp
from jax import lax
from jax.sharding import PartitionSpec as P

HEADS = 48
KV_HEADS = 8
HEAD_DIM = 128
BLOCK = 256
NEG_FILL = -1e30
CAP = 2


def slot_match(expert_ids, experts, rows_here, n_groups):
    ids = expert_ids.reshape(n_groups, rows_here, expert_ids.shape[1])
    hit = jnp.any(ids[None, :, :, :] == experts[:, None, None, None], axis=-1)
    rank = jnp.cumsum(hit.astype(jnp.int32), axis=-1) - 1
    slot = jnp.arange(CAP, dtype=jnp.int32)
    return hit[:, :, None, :] & (rank[:, :, None, :] == slot[None, None, :, None])


def shards(
    query_rows, key_cache, value_cache, lengths, attn_gain, router, expert_ids, w_gate, w_up, w_down
):
    rows_here = query_rows.shape[0]
    span = key_cache.shape[1]
    kv_share = HEADS // KV_HEADS
    n_grp = lax.axis_size("grp")
    n_shard = lax.axis_size("shard")
    grp_id = lax.axis_index("grp")
    shard_id = lax.axis_index("shard")
    n_blocks = span // BLOCK
    query_heads = query_rows.reshape(rows_here, KV_HEADS, kv_share, HEAD_DIM)
    key_heads = key_cache.reshape(rows_here, span, KV_HEADS, HEAD_DIM)
    value_heads = value_cache.reshape(rows_here, n_blocks, BLOCK, KV_HEADS, HEAD_DIM)
    scores = jnp.einsum(
        "rgjd,rtgd->rgjt", query_heads, key_heads, preferred_element_type=jnp.float32
    ) / math.sqrt(HEAD_DIM)
    position = shard_id * span + jnp.arange(span, dtype=jnp.int32)
    live_mask = (position[None, :] < lengths[:, None])[:, None, None, :]
    scores = jnp.where(live_mask, scores, NEG_FILL)
    scores = scores.reshape(rows_here, KV_HEADS, kv_share, n_blocks, BLOCK)
    live_blocks = live_mask.reshape(rows_here, 1, 1, n_blocks, BLOCK)
    block_max = jnp.max(scores, axis=-1)
    block_probs = jnp.where(live_blocks, jnp.exp(scores - block_max[..., None]), 0.0).astype(
        jnp.bfloat16
    )
    block_sum = jnp.sum(block_probs.astype(jnp.float32), axis=-1)
    block_mix = jnp.einsum(
        "rgjbt,rbtgd->rgjbd", block_probs, value_heads, preferred_element_type=jnp.float32
    )
    dev_max = jnp.max(block_max, axis=-1)
    dev_factor = jnp.exp(block_max - dev_max[..., None])
    dev_sum = jnp.sum(block_sum * dev_factor, axis=-1).reshape(rows_here, HEADS)
    dev_mix = jnp.sum(block_mix * dev_factor[..., None], axis=-2).reshape(
        rows_here, HEADS, HEAD_DIM
    )
    dev_max = dev_max.reshape(rows_here, HEADS)
    per_chunk = HEADS // n_shard
    mix_out = dev_mix.reshape(rows_here, n_shard, per_chunk, HEAD_DIM)
    side = jnp.concatenate(
        [
            dev_max.reshape(rows_here, n_shard, per_chunk),
            dev_sum.reshape(rows_here, n_shard, per_chunk),
        ],
        axis=-1,
    )
    side = jnp.pad(side, ((0, 0), (0, 0), (0, HEAD_DIM - 2 * per_chunk)))
    packed = jnp.concatenate([mix_out, side[:, :, None, :]], axis=2)
    packed = jnp.transpose(packed, (1, 0, 2, 3))
    stats = lax.all_to_all(packed, "shard", 0, 0, tiled=True)
    got_mix = stats[:, :, :per_chunk, :]
    got_max = stats[:, :, per_chunk, :per_chunk]
    got_sum = stats[:, :, per_chunk, per_chunk : 2 * per_chunk]
    top = jnp.max(got_max, axis=0)
    factor = jnp.exp(got_max - top[None])
    whole_sum = jnp.sum(got_sum * factor, axis=0)
    whole_mix = jnp.sum(got_mix * factor[..., None], axis=0)
    chunk = (whole_mix / whole_sum[..., None]).reshape(rows_here, per_chunk * HEAD_DIM)
    n_dev = n_grp * n_shard
    spread = jnp.broadcast_to(chunk.astype(jnp.bfloat16)[None], (n_dev,) + chunk.shape)
    gathered = lax.all_to_all(spread, ("grp", "shard"), 0, 0, tiled=True).astype(jnp.float32)
    gathered = gathered.reshape(n_grp, n_shard, rows_here, per_chunk * HEAD_DIM)
    attended = jnp.transpose(gathered, (0, 2, 1, 3)).reshape(n_grp * rows_here, -1)
    mean_square = jnp.mean(attended * attended, axis=-1, keepdims=True)
    normed_all = (attended * lax.rsqrt(mean_square + 1e-05) * attn_gain).astype(jnp.bfloat16)
    normed = lax.dynamic_slice_in_dim(normed_all, grp_id * rows_here, rows_here, 0)
    logits = jnp.dot(normed_all, router, preferred_element_type=jnp.float32)
    experts = router.shape[1]
    expert_range = jnp.arange(experts, dtype=jnp.int32)
    expert_hit = expert_ids[:, :, None] == expert_range[None, None, :]
    chosen = jnp.sum(jnp.where(expert_hit, logits[:, None, :], 0.0), axis=-1)
    first_weight = jax.nn.sigmoid(chosen[:, 0] - chosen[:, 1])
    route_weight = jnp.stack([first_weight, 1.0 - first_weight], axis=1)
    local_experts = w_gate.shape[0]
    assert local_experts == 1
    width = normed_all.shape[1]
    total = jnp.zeros((n_grp * rows_here, width), jnp.float32)
    for local in range(local_experts):
        expert_index = grp_id * local_experts + local
        coefficient = jnp.sum(jnp.where(expert_ids == expert_index, route_weight, 0.0), axis=-1)
        gate_proj = jnp.dot(normed_all, w_gate[local], preferred_element_type=jnp.float32)
        up_proj = jnp.dot(normed_all, w_up[local], preferred_element_type=jnp.float32)
        hidden = (jax.nn.silu(gate_proj) * up_proj).astype(jnp.bfloat16)
        expert_y = jnp.dot(hidden, w_down[local], preferred_element_type=jnp.float32)
        total = total + coefficient[:, None] * expert_y
    out_width = width // n_shard
    sending = slot_match(expert_ids, (grp_id * local_experts)[None], rows_here, n_grp)[0]
    grouped = total.reshape(n_grp, 1, rows_here, width)
    picked = jnp.sum(jnp.where(sending[..., None], grouped, 0.0), axis=2)
    blocks = picked.reshape(n_grp, CAP, n_shard, out_width)
    blocks = jnp.transpose(blocks, (0, 2, 1, 3)).reshape(n_dev, CAP, out_width)
    arrived = lax.all_to_all(blocks.astype(jnp.bfloat16), ("grp", "shard"), 0, 0, tiled=True)
    arrived = arrived.astype(jnp.float32)
    per_expert = jnp.sum(arrived.reshape(n_grp, n_shard, CAP, out_width), axis=1)
    own_ids = lax.dynamic_slice_in_dim(expert_ids, grp_id * rows_here, rows_here, 0)
    homes = slot_match(own_ids, jnp.arange(n_grp, dtype=jnp.int32) * local_experts, rows_here, 1)[
        :, 0
    ]
    spread_back = jnp.where(homes[..., None], per_expert[:, :, None, :], 0.0)
    result = jnp.sum(spread_back, axis=(0, 1))
    return (normed, result.astype(jnp.bfloat16))


def solution(mesh):
    in_specs = (
        P("grp", None),
        P("grp", "shard", None),
        P("grp", "shard", None),
        P("grp"),
        P(),
        P(),
        P(),
        P("grp", None, "shard"),
        P("grp", None, "shard"),
        P("grp", "shard", None),
    )
    out_specs = (P("grp", None), P("grp", "shard"))
    return jax.shard_map(shards, mesh=mesh, in_specs=in_specs, out_specs=out_specs, check_vma=False)
```

profile of v0, /device:TPU:0, one launch (start us, length us, event | category | flops | bytes accessed | tf_op | source)
XLA Modules:
  0.0 63.7 jit_solution(13962101609671001244)
XLA Ops:
  0.7 1.0 %reshape.264 = bf16[4,8,6,128]{3,2,1,0:T(8,128)(2,1)S(1)} reshape(bf16[4,6144]{1,0:T(4,128)(2,1)} %param.10) | data formatting | bytes 98304 | tf_op jit(solution)/shard_map/reshape | solution.py:34
  1.7 0.9 %broadcast_compare_fusion = pred[4,256]{1,0:T(4,128)(4,1)S(1)} fusion(s32[256]{0:T(256)S(1)} %iota_add_fusion, s32[4]{0:T(128)} %param.13), kind=kLoop, calls=%fused_computation.57 | loop fusion | flops 1024 | bytes 2064 | tf_op jit(solution)/shard_map/lt | solution.py:41
  2.6 0.7 %fusion.56 = (f32[4,8,6]{2,1,0:T(8,128)S(1)}, f32[4,8,6,256]{3,2,1,0:T(8,128)S(1)}) fusion(bf16[4,8,6,128]{3,2,1,0:T(8,128)(2,1)S(1)} %reshape.264, pred[4,256]{1,0:T(4,128)(4,1)S(1)} %broadcast_compare_fusion, bf16[4,256,1024]{2,1,0:T(8,128)(2,1)S(1)} %copy-done), kind=kOutput, calls=%fused_computation.72 | convolution fusion | flops 12730176 | bytes 2344704 | tf_op jit(solution)/shard_map/rgjd,rtgd->rgjt/dot_general | solution.py:37
  3.3 0.2 convert_reduce_fusion
  3.6 0.4 fusion.27
  4.1 0.7 %copy.82 = f32[8,4,7,128]{3,1,2,0:T(4,128)} copy(f32[8,4,7,128]{3,2,0,1:T(8,128)S(1)} %maximum_bitcast_fusion) | data formatting | bytes 229376 | tf_op jit(solution)/shard_map/transpose | solution.py:71
  4.8 7.4 %all-to-all-start = ((f32[8,4,7,128]{3,1,2,0:T(4,128)}), f32[8,4,7,128]{3,1,2,0:T(4,128)S(1)}, u32[]{:S(2)}, u32[]{:S(2)}) async-start(f32[8,4,7,128]{3,1,2,0:T(4,128)} %copy.82), calls=%async_computation | async-start | bytes 229376 | tf_op jit(solution)/shard_map/all_to_all | solution.py:72
  12.4 0.2 reduce_window_sum.23
  12.6 0.2 reduce_window_sum.22
  12.8 6.6 %all-to-all-done = f32[8,4,7,128]{3,1,2,0:T(4,128)S(1)} async-done(((f32[8,4,7,128]{3,1,2,0:T(4,128)}), f32[8,4,7,128]{3,1,2,0:T(4,128)S(1)}, u32[]{:S(2)}, u32[]{:S(2)}) %all-to-all-start) | async-done | bytes 114720 | tf_op jit(solution)/shard_map/all_to_all | solution.py:72
  19.5 0.1 fusion.46
  19.6 0.1 copy.84
  19.7 0.1 copy.85
  19.8 0.1 fusion.38
  20.0 0.7 %broadcast_in_dim.116 = bf16[32,4,768]{2,1,0:T(4,128)(2,1)} broadcast(bf16[4,768]{1,0:T(4,128)(2,1)S(1)} %fusion.48), dimensions={1,2} | broadcast | bytes 202752 | tf_op jit(solution)/shard_map/broadcast_in_dim | solution.py:82
  20.7 2.6 %all-to-all-start.1 = ((bf16[32,4,768]{2,1,0:T(4,128)(2,1)}), bf16[32,4,768]{2,1,0:T(4,128)(2,1)S(1)}, u32[]{:S(2)}, u32[]{:S(2)}) async-start(bf16[32,4,768]{2,1,0:T(4,128)(2,1)} %broadcast_in_dim.116), calls=%async_computation.1 | async-start | bytes 393216 | tf_op jit(solution)/shard_map/all_to_all | solution.py:83
  23.3 8.5 %all-to-all-done.1 = bf16[32,4,768]{2,1,0:T(4,128)(2,1)S(1)} async-done(((bf16[32,4,768]{2,1,0:T(4,128)(2,1)}), bf16[32,4,768]{2,1,0:T(4,128)(2,1)S(1)}, u32[]{:S(2)}, u32[]{:S(2)}) %all-to-all-start.1) | async-done | bytes 196640 | tf_op jit(solution)/shard_map/all_to_all | solution.py:83
  31.9 0.1 copy.98
  32.1 0.1 multiply_reduce_fusion
  32.2 0.1 copy.88
  32.4 0.1 multiply_convert_fusion.1
  32.5 0.2 fusion.57
  32.7 0.1 multiply_convert_fusion
  33.0 6.3 %fusion.4 = f32[16,1024]{1,0:T(8,128)S(1)} fusion(bf16[16,6144]{1,0:T(8,128)(2,1)S(1)} %bitcast.104, bf16[1,6144,1024]{2,1,0:T(8,128)(2,1)} %param.17), kind=kOutput, calls=%fused_computation.4 | convolution fusion | flops 201326592 | bytes 12845056 | tf_op jit(solution)/shard_map/dot_general | solution.py:103
  39.3 11.5 %fusion.6 = f32[16,6144]{1,0:T(8,128)S(1)} fusion(bf16[1,1024,6144]{2,1,0:T(8,128)(2,1)} %param.19, bf16[16,6144]{1,0:T(8,128)(2,1)S(1)} %bitcast.105, bf16[1,6144,1024]{2,1,0:T(8,128)(2,1)} %param.18, f32[16]{0:T(128)S(1)} %fusion.50, f32[16,1024]{1,0:T(8,128)S(1)} %fusion.4), kind=kOutput, calls=%fused_computation.6 | convolution fusion | flops 402849792 | bytes 25821248 | tf_op jit(solution)/shard_map/dot_general | solution.py:106
  50.8 0.1 broadcast_in_dim.122
  50.9 0.6 select_reduce_fusion
  51.7 0.7 %copy.91 = bf16[32,2,768]{2,1,0:T(2,128)(2,1)} copy(bf16[32,2,768]{2,0,1:T(8,128)(2,1)S(1)} %bitcast.109) | data formatting | bytes 196608 | tf_op jit(solution)/shard_map/convert_element_type | solution.py:114
  52.4 2.9 %all-to-all-start.2 = ((bf16[32,2,768]{2,1,0:T(2,128)(2,1)}), bf16[32,2,768]{2,1,0:T(2,128)(2,1)S(1)}, u32[]{:S(2)}, u32[]{:S(2)}) async-start(bf16[32,2,768]{2,1,0:T(2,128)(2,1)} %copy.91), calls=%async_computation.2 | async-start | bytes 196608 | tf_op jit(solution)/shard_map/all_to_all | solution.py:114
  55.3 0.7 %constant_dynamic-slice_fusion.1 = bf16[4,6144]{1,0:T(4,128)(2,1)} fusion(bf16[16,6144]{1,0:T(8,128)(2,1)S(1)} %multiply_convert_fusion.1, s32[]{:T(128)S(6)} %select_n.31), kind=kLoop, calls=%fused_computation.66 | loop fusion | bytes 98308 | tf_op jit(solution)/shard_map/dynamic_slice | solution.py:88
  56.0 6.9 %all-to-all-done.2 = bf16[32,2,768]{2,1,0:T(2,128)(2,1)S(1)} async-done(((bf16[32,2,768]{2,1,0:T(2,128)(2,1)}), bf16[32,2,768]{2,1,0:T(2,128)(2,1)S(1)}, u32[]{:S(2)}, u32[]{:S(2)}) %all-to-all-start.2) | async-done | bytes 98336 | tf_op jit(solution)/shard_map/all_to_all | solution.py:114
  63.0 0.7 %select_reduce_fusion.1 = bf16[4,768]{1,0:T(4,128)(2,1)} fusion(f32[4,2,768]{2,1,0:T(2,128)S(1)} %convert_reduce_fusion.1, pred[4,2,4]{2,1,0:T(4,128)(4,1)S(1)} %compare_and_fusion.1), kind=kLoop, calls=%fused_computation.32 | loop fusion | flops 46080 | bytes 30752 | tf_op jit(solution)/shard_map/reduce_sum | solution.py:122
  (39 shorter events, 0.9 us)
Async XLA Ops:
  0.6 1.9 %copy-start = (bf16[4,256,1024]{2,1,0:T(8,128)(2,1)S(1)}, bf16[4,256,1024]{2,1,0:T(8,128)(2,1)}, u32[]{:S(2)}) copy-start(bf16[4,256,1024]{2,1,0:T(8,128)(2,1)} %param.11) | copy-start | bytes 6291460
  1.7 1.9 %copy-start.1 = (bf16[4,256,1024]{2,1,0:T(8,128)(2,1)S(1)}, bf16[4,256,1024]{2,1,0:T(8,128)(2,1)}, u32[]{:S(2)}) copy-start(bf16[4,256,1024]{2,1,0:T(8,128)(2,1)} %param.12) | copy-start | bytes 6291460
  3.3 8.9 %copy-start.2 = (f32[6144]{0:T(1024)S(1)}, f32[6144]{0:T(1024)}, u32[]{:S(2)}) copy-start(f32[6144]{0:T(1024)} %param.14) | copy-start | bytes 73732
  3.3 8.9 %copy-start.3 = (s32[16,2]{0,1:T(2,128)S(1)}, s32[16,2]{0,1:T(2,128)}, u32[]{:S(2)}) copy-start(s32[16,2]{0,1:T(2,128)} %param.16) | copy-start | bytes 388
  4.8 27.7 %copy-start.4 = (bf16[6144,4]{0,1:T(4,128)(2,1)S(1)}, bf16[6144,4]{0,1:T(4,128)(2,1)}, u32[]{:S(2)}) copy-start(bf16[6144,4]{0,1:T(4,128)(2,1)} %param.15) | copy-start | bytes 147460
  4.8 14.6 %all-to-all-start = ((f32[8,4,7,128]{3,1,2,0:T(4,128)}), f32[8,4,7,128]{3,1,2,0:T(4,128)S(1)}, u32[]{:S(2)}, u32[]{:S(2)}) async-start(f32[8,4,7,128]{3,1,2,0:T(4,128)} %copy.82), calls=%async_computation | async-start | bytes 229376 | tf_op jit(solution)/shard_map/all_to_all | solution.py:72
  20.7 11.1 %all-to-all-start.1 = ((bf16[32,4,768]{2,1,0:T(4,128)(2,1)}), bf16[32,4,768]{2,1,0:T(4,128)(2,1)S(1)}, u32[]{:S(2)}, u32[]{:S(2)}) async-start(bf16[32,4,768]{2,1,0:T(4,128)(2,1)} %broadcast_in_dim.116), calls=%async_computation.1 | async-start | bytes 393216 | tf_op jit(solution)/shard_map/all_to_all | solution.py:83
  52.4 10.5 %all-to-all-start.2 = ((bf16[32,2,768]{2,1,0:T(2,128)(2,1)}), bf16[32,2,768]{2,1,0:T(2,128)(2,1)S(1)}, u32[]{:S(2)}, u32[]{:S(2)}) async-start(bf16[32,2,768]{2,1,0:T(2,128)(2,1)} %copy.91), calls=%async_computation.2 | async-start | bytes 196608 | tf_op jit(solution)/shard_map/all_to_all | solution.py:114
where the time goes:
time: 64.1 us; the launch traced here: 63.7 us
  waiting for transfers between devices  22 us (34%)
  matrix products  19.2 us (30%)
  starting transfers between devices  12.9 us (20%)
  local copies, waits for them, and re-layouts  4.82 us (8%)
  other arithmetic  3.87 us (6%)
  between operations  0.87 us (1%)
    dot_general x1, matrix products, shards(): jnp.dot(hidden, w_down[local], preferred_element_type=jnp.float32)  11.5 us
    all_to_all x1, waiting for transfers between devices, shards(): lax.all_to_all(spread, ('grp', 'shard'), 0, 0, tiled=True)  8.52 us
    all_to_all x1, starting transfers between devices, shards(): stats = lax.all_to_all(packed, 'shard', 0, 0, tiled=True)  7.38 us
    all_to_all x1, waiting for transfers between devices, shards(): lax.all_to_all(blocks.astype(jnp.bfloat16), ('grp', 'shard'), 0, 0, tiled...  6.9 us
    all_to_all x1, waiting for transfers between devices, shards(): stats = lax.all_to_all(packed, 'shard', 0, 0, tiled=True)  6.61 us
    dot_general x1, matrix products, shards(): jnp.dot(normed_all, w_gate[local], preferred_element_type=jnp.float32)  6.3 us
    all_to_all x1, starting transfers between devices, shards(): lax.all_to_all(blocks.astype(jnp.bfloat16), ('grp', 'shard'), 0, 0, tiled...  2.95 us
    all_to_all x1, starting transfers between devices, shards(): lax.all_to_all(spread, ('grp', 'shard'), 0, 0, tiled=True)  2.58 us
  transfers between devices with their start and end apart: 3, of which 3 were waited for; matrix products, arithmetic and copies ran while one was open for 2% of the time, Pallas kernels for 0%

commit v1 on v0

--- a/solution.py
+++ b/solution.py
@@ -10,6 +10,17 @@
 BLOCK = 256
 NEG_FILL = -1e30
 CAP = 2
+
+
+def in_blocks(x, dim, count):
+    before, after = (x.shape[:dim], x.shape[dim + 1 :])
+    return jnp.moveaxis(x.reshape(*before, count, -1, *after), dim, 0)
+
+
+def in_order(parts, dim):
+    dims = list(parts.shape[1:])
+    dims[dim] *= parts.shape[0]
+    return jnp.moveaxis(parts, 0, dim).reshape(dims)
 
 
 def slot_match(expert_ids, experts, rows_here, n_groups):
@@ -69,7 +80,14 @@
     side = jnp.pad(side, ((0, 0), (0, 0), (0, HEAD_DIM - 2 * per_chunk)))
     packed = jnp.concatenate([mix_out, side[:, :, None, :]], axis=2)
     packed = jnp.transpose(packed, (1, 0, 2, 3))
-    stats = lax.all_to_all(packed, "shard", 0, 0, tiled=True)
+    size, here = (lax.axis_size("shard"), lax.axis_index("shard"))
+    pieces = in_blocks(packed, 0, size)
+    finished = [pieces[here]]
+    for lap in range(1, size):
+        sent = pieces[here ^ lap]
+        finished.append(lax.ppermute(sent, "shard", [(i, i ^ lap) for i in range(size)]))
+    pieces = jnp.stack(finished)[here ^ jnp.arange(size)]
+    stats = in_order(pieces, 0)
     got_mix = stats[:, :, :per_chunk, :]
     got_max = stats[:, :, per_chunk, :per_chunk]
     got_sum = stats[:, :, per_chunk, per_chunk : 2 * per_chunk]

time: 64.1 us -> 70.4 us (1.098)
  starting transfers between devices: 12.9 us -> 18.1 us
  matrix products: 19.2 us -> 20.8 us
    ppermute x0 -> x7, starting transfers between devices: none -> 12.6 us  [shards(): lax.ppermute(sent, 'shard', [(i, i ^ lap) for i in range(size)])]
    all_to_all x1 -> x0, starting transfers between devices: 7.38 us -> none  [shards(): stats = lax.all_to_all(packed, 'shard', 0, 0, tiled=True)]
    all_to_all x1 -> x0, waiting for transfers between devices: 6.61 us -> none  [shards(): stats = lax.all_to_all(packed, 'shard', 0, 0, tiled=True)]
    ppermute x0 -> x7, waiting for transfers between devices: none -> 6.31 us  [shards(): lax.ppermute(sent, 'shard', [(i, i ^ lap) for i in range(size)])]
    dot_general x1, matrix products: 0.43 us -> 2.01 us  [shards(): jnp.einsum('rgjbt,rbtgd->rgjbd', block_probs, value_heads, preferred_elem...]
    transpose x1 -> x0, local copies, waits for them, and re-layouts: 0.71 us -> none  [shards(): packed = jnp.transpose(packed, (1, 0, 2, 3))]
  transfers between devices with their start and end apart: 3 -> 9, of which waited for: 3 -> 4; matrix products, arithmetic and copies ran while one was open for 2% -> 2% of each run, Pallas kernels for 0% -> 0%
where the time goes in v1:
time: 70.4 us; the launch traced here: 70.1 us
  waiting for transfers between devices  21.7 us (31%)
  matrix products  20.8 us (30%)
  starting transfers between devices  18.1 us (26%)
  local copies, waits for them, and re-layouts  4.82 us (7%)
  other arithmetic  3.73 us (5%)
  between operations  0.99 us (1%)
    ppermute x7, starting transfers between devices, shards(): lax.ppermute(sent, 'shard', [(i, i ^ lap) for i in range(size)])  12.6 us
    dot_general x1, matrix products, shards(): jnp.dot(hidden, w_down[local], preferred_element_type=jnp.float32)  11.5 us
    all_to_all x1, waiting for transfers between devices, shards(): lax.all_to_all(spread, ('grp', 'shard'), 0, 0, tiled=True)  8.51 us
    all_to_all x1, waiting for transfers between devices, shards(): lax.all_to_all(blocks.astype(jnp.bfloat16), ('grp', 'shard'), 0, 0, tiled...  6.9 us
    dot_general x1, matrix products, shards(): jnp.dot(normed_all, w_gate[local], preferred_element_type=jnp.float32)  6.31 us
    ppermute x7, waiting for transfers between devices, shards(): lax.ppermute(sent, 'shard', [(i, i ^ lap) for i in range(size)])  6.31 us
    all_to_all x1, starting transfers between devices, shards(): lax.all_to_all(blocks.astype(jnp.bfloat16), ('grp', 'shard'), 0, 0, tiled...  2.95 us
    all_to_all x1, starting transfers between devices, shards(): lax.all_to_all(spread, ('grp', 'shard'), 0, 0, tiled=True)  2.58 us
  transfers between devices with their start and end apart: 9, of which 4 were waited for; matrix products, arithmetic and copies ran while one was open for 2% of the time, Pallas kernels for 0%

profile of v1, /device:TPU:0, one launch (start us, length us, event | category | flops | bytes accessed | tf_op | source)
XLA Modules:
  0.0 70.1 jit_solution(1269426190407753620)
XLA Ops:
  0.7 1.0 %reshape.308 = bf16[4,8,6,128]{3,2,1,0:T(8,128)(2,1)S(1)} reshape(bf16[4,6144]{1,0:T(4,128)(2,1)} %param.10) | data formatting | bytes 98304 | tf_op jit(solution)/shard_map/reshape | solution.py:45
  1.7 0.7 %broadcast_compare_fusion = pred[4,256]{1,0:T(4,128)(4,1)S(1)} fusion(s32[256]{0:T(256)S(1)} %iota_add_fusion, s32[4]{0:T(128)} %param.13), kind=kLoop, calls=%fused_computation.101 | loop fusion | flops 1024 | bytes 2064 | tf_op jit(solution)/shard_map/lt | solution.py:52
  2.4 0.7 %fusion.66 = (f32[4,8,6]{2,1,0:T(8,128)S(1)}, f32[4,8,6,256]{3,2,1,0:T(8,128)S(1)}) fusion(bf16[4,8,6,128]{3,2,1,0:T(8,128)(2,1)S(1)} %reshape.308, pred[4,256]{1,0:T(4,128)(4,1)S(1)} %broadcast_compare_fusion, bf16[4,256,1024]{2,1,0:T(8,128)(2,1)S(1)} %copy-done), kind=kOutput, calls=%fused_computation.115 | convolution fusion | flops 12730176 | bytes 2344704 | tf_op jit(solution)/shard_map/rgjd,rtgd->rgjt/dot_general | solution.py:48
  3.2 0.2 convert_reduce_fusion
  3.5 2.0 %fusion.27 = f32[4,8,6,128]{3,2,1,0:T(8,128)S(1)} fusion(f32[4,8,6]{2,1,0:T(8,128)S(1)} %get-tuple-element.15, f32[4,8,6,256]{3,2,1,0:T(8,128)S(1)} %get-tuple-element.17, f32[4,8,6]{2,1,0:T(8,128)S(1)} %get-tuple-element.16, pred[4,256]{1,0:T(4,128)(4,1)S(1)} %broadcast_compare_fusion, bf16[4,256,1024]{2,1,0:T(8,128)(2,1)} %param.12), kind=kOutput, calls=%fused_computation.18 | convolution fusion | flops 12754944 | bytes 2394624 | tf_op jit(solution)/shard_map/rgjbt,rbtgd->rgjbd/dot_general | solution.py:61
  5.6 3.0 %collective-permute-start = (f32[1,4,7,128]{3,1,2,0:T(4,128)S(1)}, f32[1,4,7,128]{3,1,2,0:T(4,128)S(1)}, u32[]{:S(2)}, u32[]{:S(2)}) collective-permute-start(f32[1,4,7,128]{3,1,2,0:T(4,128)S(1)} %bitcast.153), channel_id=1, source_target_pairs={{0,1},{1,0},{2,3},{3,2},{4,5},{5,4},{6,7},{7,6},{8,9},{9,8},{10,11... | collective-permute-start | bytes 43016 | tf_op jit(solution)/shard_map/ppermute | solution.py:88
  8.6 1.6 %collective-permute-start.1 = (f32[1,4,7,128]{3,1,2,0:T(4,128)S(1)}, f32[1,4,7,128]{3,1,2,0:T(4,128)S(1)}, u32[]{:S(2)}, u32[]{:S(2)}) collective-permute-start(f32[1,4,7,128]{3,1,2,0:T(4,128)S(1)} %bitcast.152), channel_id=1, source_target_pairs={{0,2},{1,3},{2,0},{3,1},{4,6},{5,7},{6,4},{7,5},{8,10},{9,11},{10,... | collective-permute-start | bytes 43016 | tf_op jit(solution)/shard_map/ppermute | solution.py:88
  10.2 3.0 %collective-permute-start.3 = (f32[1,4,7,128]{3,1,2,0:T(4,128)S(1)}, f32[1,4,7,128]{3,1,2,0:T(4,128)S(1)}, u32[]{:S(2)}, u32[]{:S(2)}) collective-permute-start(f32[1,4,7,128]{3,1,2,0:T(4,128)S(1)} %bitcast.150), channel_id=1, source_target_pairs={{0,4},{1,5},{2,6},{3,7},{4,0},{5,1},{6,2},{7,3},{8,12},{9,13},{10,... | collective-permute-start | bytes 43016 | tf_op jit(solution)/shard_map/ppermute | solution.py:88
  13.2 1.3 %collective-permute-start.4 = (f32[1,4,7,128]{3,1,2,0:T(4,128)S(1)}, f32[1,4,7,128]{3,1,2,0:T(4,128)S(1)}, u32[]{:S(2)}, u32[]{:S(2)}) collective-permute-start(f32[1,4,7,128]{3,1,2,0:T(4,128)S(1)} %bitcast.154), channel_id=1, source_target_pairs={{0,5},{1,4},{2,7},{3,6},{4,1},{5,0},{6,3},{7,2},{8,13},{9,12},{10,... | collective-permute-start | bytes 43016 | tf_op jit(solution)/shard_map/ppermute | solution.py:88
  14.7 0.2 reduce_window_sum.23
  15.0 0.2 reduce_window_sum.22
  15.2 3.6 %collective-permute-start.5 = (f32[1,4,7,128]{3,1,2,0:T(4,128)S(1)}, f32[1,4,7,128]{3,1,2,0:T(4,128)S(1)}, u32[]{:S(2)}, u32[]{:S(2)}) collective-permute-start(f32[1,4,7,128]{3,1,2,0:T(4,128)S(1)} %bitcast.156), channel_id=1, source_target_pairs={{0,6},{1,7},{2,4},{3,5},{4,2},{5,3},{6,0},{7,1},{8,14},{9,15},{10,... | collective-permute-start | bytes 43016 | tf_op jit(solution)/shard_map/ppermute | solution.py:88
  19.0 1.8 %collective-permute-done.5 = f32[1,4,7,128]{3,1,2,0:T(4,128)S(1)} collective-permute-done((f32[1,4,7,128]{3,1,2,0:T(4,128)S(1)}, f32[1,4,7,128]{3,1,2,0:T(4,128)S(1)}, u32[]{:S(2)}, u32[]{:S(2)}) %collective-permute-start.5) | collective-permute-done | bytes 14368 | tf_op jit(solution)/shard_map/ppermute | solution.py:88
  20.8 4.5 %collective-permute-done.6 = f32[1,4,7,128]{3,1,2,0:T(4,128)S(1)} collective-permute-done((f32[1,4,7,128]{3,1,2,0:T(4,128)S(1)}, f32[1,4,7,128]{3,1,2,0:T(4,128)S(1)}, u32[]{:S(2)}, u32[]{:S(2)}) %collective-permute-start.6) | collective-permute-done | bytes 14368 | tf_op jit(solution)/shard_map/ppermute | solution.py:88
  25.3 0.6 gather_fusion
  26.0 0.1 copy.104
  26.1 0.1 fusion.38
  26.4 0.7 %broadcast_in_dim.117 = bf16[32,4,768]{2,1,0:T(4,128)(2,1)} broadcast(bf16[4,768]{1,0:T(4,128)(2,1)S(1)} %fusion.57), dimensions={1,2} | broadcast | bytes 202752 | tf_op jit(solution)/shard_map/broadcast_in_dim | solution.py:100
  27.2 2.6 %all-to-all-start = ((bf16[32,4,768]{2,1,0:T(4,128)(2,1)}), bf16[32,4,768]{2,1,0:T(4,128)(2,1)S(1)}, u32[]{:S(2)}, u32[]{:S(2)}) async-start(bf16[32,4,768]{2,1,0:T(4,128)(2,1)} %broadcast_in_dim.117), calls=%async_computation | async-start | bytes 393216 | tf_op jit(solution)/shard_map/all_to_all | solution.py:101
  29.8 8.5 %all-to-all-done = bf16[32,4,768]{2,1,0:T(4,128)(2,1)S(1)} async-done(((bf16[32,4,768]{2,1,0:T(4,128)(2,1)}), bf16[32,4,768]{2,1,0:T(4,128)(2,1)S(1)}, u32[]{:S(2)}, u32[]{:S(2)}) %all-to-all-start) | async-done | bytes 196640 | tf_op jit(solution)/shard_map/all_to_all | solution.py:101
  38.4 0.1 copy.121
  38.5 0.1 multiply_reduce_fusion
  38.8 0.1 multiply_convert_fusion
  39.1 0.2 fusion.67
  39.4 6.3 %fusion.4 = f32[16,1024]{1,0:T(8,128)S(1)} fusion(bf16[16,6144]{1,0:T(8,128)(2,1)S(1)} %bitcast.141, bf16[1,6144,1024]{2,1,0:T(8,128)(2,1)} %param.17), kind=kOutput, calls=%fused_computation.5 | convolution fusion | flops 201326592 | bytes 12845056 | tf_op jit(solution)/shard_map/dot_general | solution.py:121
  45.7 11.5 %fusion.6 = f32[16,6144]{1,0:T(8,128)S(1)} fusion(bf16[1,1024,6144]{2,1,0:T(8,128)(2,1)} %param.19, bf16[16,6144]{1,0:T(8,128)(2,1)S(1)} %bitcast.142, bf16[1,6144,1024]{2,1,0:T(8,128)(2,1)} %param.18, f32[16]{0:T(128)S(1)} %fusion.59, f32[16,1024]{1,0:T(8,128)S(1)} %fusion.4), kind=kOutput, calls=%fused_computation.7 | convolution fusion | flops 402849792 | bytes 25821248 | tf_op jit(solution)/shard_map/dot_general | solution.py:124
  57.4 0.6 select_reduce_fusion
  58.1 0.7 %copy.112 = bf16[32,2,768]{2,1,0:T(2,128)(2,1)} copy(bf16[32,2,768]{2,0,1:T(8,128)(2,1)S(1)} %bitcast.146) | data formatting | bytes 196608 | tf_op jit(solution)/shard_map/convert_element_type | solution.py:132
  58.8 2.9 %all-to-all-start.1 = ((bf16[32,2,768]{2,1,0:T(2,128)(2,1)}), bf16[32,2,768]{2,1,0:T(2,128)(2,1)S(1)}, u32[]{:S(2)}, u32[]{:S(2)}) async-start(bf16[32,2,768]{2,1,0:T(2,128)(2,1)} %copy.112), calls=%async_computation.1 | async-start | bytes 196608 | tf_op jit(solution)/shard_map/all_to_all | solution.py:132
  61.8 0.7 constant_dynamic-slice_fusion.1
  62.4 6.9 %all-to-all-done.1 = bf16[32,2,768]{2,1,0:T(2,128)(2,1)S(1)} async-done(((bf16[32,2,768]{2,1,0:T(2,128)(2,1)}), bf16[32,2,768]{2,1,0:T(2,128)(2,1)S(1)}, u32[]{:S(2)}, u32[]{:S(2)}) %all-to-all-start.1) | async-done | bytes 98336 | tf_op jit(solution)/shard_map/all_to_all | solution.py:132
  69.4 0.7 select_reduce_fusion.1
  (67 shorter events, 1.7 us)
Async XLA Ops:
  0.6 1.8 %copy-start = (bf16[4,256,1024]{2,1,0:T(8,128)(2,1)S(1)}, bf16[4,256,1024]{2,1,0:T(8,128)(2,1)}, u32[]{:S(2)}) copy-start(bf16[4,256,1024]{2,1,0:T(8,128)(2,1)} %param.11) | copy-start | bytes 6291460
  3.1 11.4 %copy-start.2 = (s32[16,2]{0,1:T(2,128)S(1)}, s32[16,2]{0,1:T(2,128)}, u32[]{:S(2)}) copy-start(s32[16,2]{0,1:T(2,128)} %param.16) | copy-start | bytes 388
  3.2 11.9 %copy-start.1 = (f32[6144]{0:T(1024)S(1)}, f32[6144]{0:T(1024)}, u32[]{:S(2)}) copy-start(f32[6144]{0:T(1024)} %param.14) | copy-start | bytes 73732
  5.6 9.7 %collective-permute-start = (f32[1,4,7,128]{3,1,2,0:T(4,128)S(1)}, f32[1,4,7,128]{3,1,2,0:T(4,128)S(1)}, u32[]{:S(2)}, u32[]{:S(2)}) collective-permute-start(f32[1,4,7,128]{3,1,2,0:T(4,128)S(1)} %bitcast.153), channel_id=1, source_target_pairs={{0,1},{1,0},{2,3},{3,2},{4,5},{5,4},{6,7},{7,6},{8,9},{9,8},{10,11... | collective-permute-start | bytes 43016 | tf_op jit(solution)/shard_map/ppermute | solution.py:88
  8.6 10.3 %collective-permute-start.1 = (f32[1,4,7,128]{3,1,2,0:T(4,128)S(1)}, f32[1,4,7,128]{3,1,2,0:T(4,128)S(1)}, u32[]{:S(2)}, u32[]{:S(2)}) collective-permute-start(f32[1,4,7,128]{3,1,2,0:T(4,128)S(1)} %bitcast.152), channel_id=1, source_target_pairs={{0,2},{1,3},{2,0},{3,1},{4,6},{5,7},{6,4},{7,5},{8,10},{9,11},{10,... | collective-permute-start | bytes 43016 | tf_op jit(solution)/shard_map/ppermute | solution.py:88
  10.2 8.7 %collective-permute-start.2 = (f32[1,4,7,128]{3,1,2,0:T(4,128)S(1)}, f32[1,4,7,128]{3,1,2,0:T(4,128)S(1)}, u32[]{:S(2)}, u32[]{:S(2)}) collective-permute-start(f32[1,4,7,128]{3,1,2,0:T(4,128)S(1)} %bitcast.151), channel_id=1, source_target_pairs={{0,3},{1,2},{2,1},{3,0},{4,7},{5,6},{6,5},{7,4},{8,11},{9,10},{10,... | collective-permute-start | bytes 43016 | tf_op jit(solution)/shard_map/ppermute | solution.py:88
  10.2 8.7 %collective-permute-start.3 = (f32[1,4,7,128]{3,1,2,0:T(4,128)S(1)}, f32[1,4,7,128]{3,1,2,0:T(4,128)S(1)}, u32[]{:S(2)}, u32[]{:S(2)}) collective-permute-start(f32[1,4,7,128]{3,1,2,0:T(4,128)S(1)} %bitcast.150), channel_id=1, source_target_pairs={{0,4},{1,5},{2,6},{3,7},{4,0},{5,1},{6,2},{7,3},{8,12},{9,13},{10,... | collective-permute-start | bytes 43016 | tf_op jit(solution)/shard_map/ppermute | solution.py:88
  13.2 5.7 %collective-permute-start.4 = (f32[1,4,7,128]{3,1,2,0:T(4,128)S(1)}, f32[1,4,7,128]{3,1,2,0:T(4,128)S(1)}, u32[]{:S(2)}, u32[]{:S(2)}) collective-permute-start(f32[1,4,7,128]{3,1,2,0:T(4,128)S(1)} %bitcast.154), channel_id=1, source_target_pairs={{0,5},{1,4},{2,7},{3,6},{4,1},{5,0},{6,3},{7,2},{8,13},{9,12},{10,... | collective-permute-start | bytes 43016 | tf_op jit(solution)/shard_map/ppermute | solution.py:88
  15.2 5.5 %collective-permute-start.5 = (f32[1,4,7,128]{3,1,2,0:T(4,128)S(1)}, f32[1,4,7,128]{3,1,2,0:T(4,128)S(1)}, u32[]{:S(2)}, u32[]{:S(2)}) collective-permute-start(f32[1,4,7,128]{3,1,2,0:T(4,128)S(1)} %bitcast.156), channel_id=1, source_target_pairs={{0,6},{1,7},{2,4},{3,5},{4,2},{5,3},{6,0},{7,1},{8,14},{9,15},{10,... | collective-permute-start | bytes 43016 | tf_op jit(solution)/shard_map/ppermute | solution.py:88
  18.8 6.4 %collective-permute-start.6 = (f32[1,4,7,128]{3,1,2,0:T(4,128)S(1)}, f32[1,4,7,128]{3,1,2,0:T(4,128)S(1)}, u32[]{:S(2)}, u32[]{:S(2)}) collective-permute-start(f32[1,4,7,128]{3,1,2,0:T(4,128)S(1)} %bitcast.155), channel_id=1, source_target_pairs={{0,7},{1,6},{2,5},{3,4},{4,3},{5,2},{6,1},{7,0},{8,15},{9,14},{10,... | collective-permute-start | bytes 43016 | tf_op jit(solution)/shard_map/ppermute | solution.py:88
  27.2 11.1 %all-to-all-start = ((bf16[32,4,768]{2,1,0:T(4,128)(2,1)}), bf16[32,4,768]{2,1,0:T(4,128)(2,1)S(1)}, u32[]{:S(2)}, u32[]{:S(2)}) async-start(bf16[32,4,768]{2,1,0:T(4,128)(2,1)} %broadcast_in_dim.117), calls=%async_computation | async-start | bytes 393216 | tf_op jit(solution)/shard_map/all_to_all | solution.py:101
  29.8 9.4 %copy-start.3 = (bf16[6144,4]{0,1:T(4,128)(2,1)S(1)}, bf16[6144,4]{0,1:T(4,128)(2,1)}, u32[]{:S(2)}) copy-start(bf16[6144,4]{0,1:T(4,128)(2,1)} %param.15) | copy-start | bytes 147460
  58.8 10.5 %all-to-all-start.1 = ((bf16[32,2,768]{2,1,0:T(2,128)(2,1)}), bf16[32,2,768]{2,1,0:T(2,128)(2,1)S(1)}, u32[]{:S(2)}, u32[]{:S(2)}) async-start(bf16[32,2,768]{2,1,0:T(2,128)(2,1)} %copy.112), calls=%async_computation.1 | async-start | bytes 196608 | tf_op jit(solution)/shard_map/all_to_all | solution.py:132
